TPU v7x, 512 devices: a whole 4x8x8 slice. The times are simulated.
512 devices in a mesh: dp: 32 (over z, x), fsdp: 16 (over y, core).
Axes of the slice: x: 4, y: 8, z: 8, core: 2. Of those that a mesh axis runs over, the one named last changes fastest.
Arguments:
- projected: bfloat16 [65536, 2304], P(('dp', 'fsdp')), may hold values from -7.03125 to 7.03125
- out_weight: bfloat16 [768, 1536], P('fsdp'), may hold values from -0.21875 to 0.21875
- kernel: float32 [31, 1536], replicated, may hold values from -2 to 2
- cotangent: bfloat16 [65536, 1536], P(('dp', 'fsdp')), may hold values from -6 to 6
- send_rows: int32 [65536], P(('dp', 'fsdp')), may hold values from -1 to 127, as said below
- compute_src: int32 [65536], P(('dp', 'fsdp')), may hold values from -1 to 127, as said below
- segment: int32 [65536], P(('dp', 'fsdp')), may hold values from -1 to 3, as said below
Outputs:
- block_out: bfloat16 [65536, 1536], P(('dp', 'fsdp'))
- projected_grad: bfloat16 [65536, 2304], P(('dp', 'fsdp'))
- out_weight_grad: float32 [768, 1536], P('fsdp')
- kernel_grad: float32 [31, 1536], replicated
Inputs may be any that keep to these rules, and one draw needn't show every extreme that they name: `send_rows`: A device's 128 entries are 32 blocks of 4, block t for index t of dp at the same fsdp index; each lists rows of the device's own block of projected, each row at most once, filled entries first in a block and -1 after them. In every draw some device of each fsdp index fills all its entries. `compute_src`: on device (t, f), a row holds s * 4 + k when it receives entry t * 4 + k of device (s, f); every filled entry of send_rows is received by exactly one row, and a row holds -1 when it receives nothing. Filled rows come first. In every draw some device of each fsdp index receives a full block from every device. On each device, rows with compute_src = -1 hold -1, the others hold segment numbers from 0 that never fall along the rows.
All inputs are finite; a program needn't handle non-finite values.
Results may differ from a plain program's by a relative error of at most 0.018.
Values may be sent and summed in bfloat16 or wider, within the bound.
No kernel may reach another device: no remote copies, remote signals or barrier semaphores. Data moves between devices by JAX's collectives and lax.ppermute only.
A program may use at most 128 MiB of HBM per device.

v0:
```python
import jax
import jax.numpy as jnp
from jax import lax
from jax.sharding import PartitionSpec as P

HEADS = 8
HEAD_DIM = 96


def split_heads(frames):
    length = frames.shape[0]
    inner_width = HEADS * HEAD_DIM
    query_part = frames[:, :inner_width].reshape(length, HEADS, HEAD_DIM)
    key_part = frames[:, inner_width : 2 * inner_width].reshape(length, HEADS, HEAD_DIM)
    value_part = frames[:, 2 * inner_width :].reshape(length, HEADS, HEAD_DIM)
    return (query_part, key_part, value_part)


def attend(frames, segment):
    query_part, key_part, value_part = split_heads(frames)
    scores = jnp.einsum(
        "qhd,khd->hqk", query_part, key_part, preferred_element_type=jnp.float32
    ) * HEAD_DIM ** (-0.5)
    inside = segment[:, None] == segment[None, :]
    scores = jnp.where(inside[None], scores, -1e30)
    highest = jnp.max(scores, axis=2, keepdims=True)
    weights = jnp.exp(scores - highest)
    soft_probs = weights / jnp.sum(weights, axis=2, keepdims=True)
    rounded = soft_probs.astype(jnp.bfloat16)
    context = jnp.einsum("hqk,khd->qhd", rounded, value_part, preferred_element_type=jnp.float32)
    return (
        context.reshape(frames.shape[0], HEADS * HEAD_DIM).astype(jnp.bfloat16),
        soft_probs,
        rounded,
    )


def attend_back(frames, soft_probs, rounded, context_grad):
    query_part, key_part, value_part = split_heads(frames)
    length = frames.shape[0]
    inner_width = HEADS * HEAD_DIM
    upstream = context_grad.reshape(length, HEADS, HEAD_DIM)
    value_grad = jnp.einsum("hqk,qhd->khd", rounded, upstream, preferred_element_type=jnp.float32)
    prob_grad = jnp.einsum("qhd,khd->hqk", upstream, value_part, preferred_element_type=jnp.float32)
    score_grad = soft_probs * (prob_grad - jnp.sum(prob_grad * soft_probs, axis=2, keepdims=True))
    score_grad = (score_grad * HEAD_DIM ** (-0.5)).astype(jnp.bfloat16)
    query_grad = jnp.einsum(
        "hqk,khd->qhd", score_grad, key_part, preferred_element_type=jnp.float32
    )
    key_grad = jnp.einsum(
        "hqk,qhd->khd", score_grad, query_part, preferred_element_type=jnp.float32
    )
    return jnp.concatenate(
        [
            query_grad.reshape(length, inner_width).astype(jnp.bfloat16),
            key_grad.reshape(length, inner_width).astype(jnp.bfloat16),
            value_grad.reshape(length, inner_width).astype(jnp.bfloat16),
        ],
        axis=1,
    )


def finish(mixed, kernel, segment):
    length = mixed.shape[0]
    tap_count = kernel.shape[0]
    half_span = (tap_count - 1) // 2
    signal = mixed.astype(jnp.float32)
    padded = jnp.pad(signal, ((half_span, half_span), (0, 0)))
    neighbours = jnp.pad(segment, (half_span, half_span), constant_values=-2)
    convolved = jnp.zeros_like(signal)
    for offset in range(tap_count):
        matching = (neighbours[offset : offset + length] == segment).astype(jnp.float32)
        convolved = (
            convolved + kernel[offset] * padded[offset : offset + length] * matching[:, None]
        )
    return signal + jax.nn.silu(convolved)


def body(projected, out_weight, kernel, cotangent, send_rows, compute_src, segment):
    row_count = projected.shape[0]
    present = send_rows >= 0
    outgoing = jnp.take(projected, jnp.maximum(send_rows, 0), axis=0)
    outgoing = jnp.where(present[:, None], outgoing, jnp.zeros_like(outgoing))
    incoming = lax.all_to_all(outgoing, "dp", split_axis=0, concat_axis=0, tiled=True)
    filled = compute_src >= 0
    frames = jnp.take(incoming, jnp.maximum(compute_src, 0), axis=0)
    frames = jnp.where(filled[:, None], frames, jnp.zeros_like(frames))
    context, soft_probs, rounded = attend(frames, segment)
    columns = context
    mixed_sums = jnp.dot(
        columns,
        lax.all_gather(out_weight, "fsdp", axis=0, tiled=True),
        preferred_element_type=jnp.float32,
    )
    mixed = mixed_sums.astype(jnp.bfloat16)
    result, pullback = jax.vjp(
        lambda signal, kernel_taps: finish(signal, kernel_taps, segment), mixed, kernel
    )
    mixed_grad, kernel_part = pullback(cotangent.astype(jnp.float32))
    columns = context
    weight_share = lax.psum_scatter(
        jnp.einsum("rc,rd->cd", columns, mixed_grad, preferred_element_type=jnp.float32).astype(
            jnp.bfloat16
        ),
        "fsdp",
        scatter_dimension=0,
        tiled=True,
    ).astype(jnp.float32)
    context_grad = jnp.einsum(
        "rd,cd->rc",
        mixed_grad,
        lax.all_gather(out_weight, "fsdp", axis=0, tiled=True),
        preferred_element_type=jnp.float32,
    ).astype(jnp.bfloat16)
    frame_grad = attend_back(frames, soft_probs, rounded, context_grad)
    slot_total = incoming.shape[0]
    back_index = jnp.where(filled, compute_src, slot_total)
    returning = jnp.zeros_like(incoming).at[back_index].set(frame_grad, mode="drop")
    arrived = lax.all_to_all(returning, "dp", split_axis=0, concat_axis=0, tiled=True)
    source_index = jnp.where(present, send_rows, row_count)
    projected_grad = jnp.zeros_like(projected).at[source_index].set(arrived, mode="drop")
    scale_factor = (row_count * lax.axis_size("dp") * lax.axis_size("fsdp")) ** (-0.5)
    kernel_f = lax.psum(kernel_part, "fsdp")
    both = dp_allreduce_a2a(
        jnp.concatenate([weight_share, kernel_f, jnp.zeros((17, 1536), jnp.float32)], axis=0)
    )
    weight_total, kernel_total = (both[:48], both[48:79])
    return (
        result.astype(jnp.bfloat16),
        projected_grad,
        weight_total * scale_factor,
        kernel_total * scale_factor,
    )


def dp_allreduce_rs_ag(x):
    n = lax.axis_size("dp")
    flat = x.reshape(n, -1)
    part = lax.psum_scatter(flat, "dp", scatter_dimension=0, tiled=True)
    return lax.all_gather(part, "dp", axis=0, tiled=True).reshape(x.shape)


def dp_allreduce_a2a(x):
    n = lax.axis_size("dp")
    flat = x.reshape(n, -1)
    got = lax.all_to_all(flat, "dp", split_axis=0, concat_axis=0, tiled=True)
    part = jnp.sum(got, axis=0, keepdims=True)
    return lax.all_gather(part, "dp", axis=0, tiled=True).reshape(x.shape)


def dp_allreduce_a2a2(x):
    n = lax.axis_size("dp")
    flat = x.reshape(n, -1)
    got = lax.all_to_all(flat, "dp", split_axis=0, concat_axis=0, tiled=True)
    part = jnp.sum(got, axis=0, keepdims=True)
    back = lax.all_to_all(
        jnp.broadcast_to(part, flat.shape), "dp", split_axis=0, concat_axis=0, tiled=True
    )
    return back.reshape(x.shape)


def solution(mesh):
    placed = (
        P(("dp", "fsdp"), None),
        P("fsdp", None),
        P(),
        P(("dp", "fsdp"), None),
        P(("dp", "fsdp")),
        P(("dp", "fsdp")),
        P(("dp", "fsdp")),
    )
    return jax.shard_map(
        body,
        mesh=mesh,
        in_specs=placed,
        out_specs=(P(("dp", "fsdp"), None), P(("dp", "fsdp"), None), P("fsdp", None), P()),
        check_vma=False,
    )
```

profile of v0, /device:TPU:24, one launch (start us, length us, event | category | flops | bytes accessed | tf_op | source)
XLA Modules:
  0.0 341.6 jit_solution(10079741374050329405)
XLA Ops:
  7.9 1.2 compare_select_fusion.1
  9.1 1.0 gather_fusion
  10.3 1.0 all_to_all.22
  11.3 13.2 %all-to-all-start = ((bf16[32,4,2304]{2,1,0:T(4,128)(2,1)}), bf16[32,4,2304]{2,1,0:T(4,128)(2,1)S(1)}, u32[]{:S(2)}, u32[]{:S(2)}) async-start(bf16[32,4,2304]{2,1,0:T(4,128)(2,1)} %all_to_all.22), calls=%async_computation | async-start | bytes 1179648 | tf_op jit(solution)/shard_map/all_to_all | solution.py:84
  26.0 17.5 %all-to-all-done = bf16[32,4,2304]{2,1,0:T(4,128)(2,1)S(1)} async-done(((bf16[32,4,2304]{2,1,0:T(4,128)(2,1)}), bf16[32,4,2304]{2,1,0:T(4,128)(2,1)S(1)}, u32[]{:S(2)}, u32[]{:S(2)}) %all-to-all-start) | async-done | bytes 589856 | tf_op jit(solution)/shard_map/all_to_all | solution.py:84
  43.6 1.0 gather_fusion.1
  45.3 1.2 fusion.40
  47.0 9.4 %all-gather.4.cloned.1.call-done = bf16[768,1536]{1,0:T(8,128)(2,1)} async-done(((bf16[48,1536]{1,0:T(8,128)(2,1)}), bf16[768,1536]{1,0:T(8,128)(2,1)}) %all-gather.4.cloned.1.call-update) | async-done | bytes 2359312 | tf_op jit(solution)/shard_map/all_gather | solution.py:92
  56.4 2.2 fusion.2
  58.6 7.6 %multiply_reduce_fusion.31 = (f32[1536]{0:T(1024)}, f32[1536]{0:T(1024)}, f32[1536]{0:T(1024)}, f32[1536]{0:T(1024)}, f32[1536]{0:T(1024)}, /*index=5*/f32[1536]...) fusion(f32[128,1536]{1,0:T(8,128)S(1)} %fusion.2, ...), kind=kLoop, calls=%fused_computation.99 | loop fusion | flops 25152000 | bytes 3013632 | tf_op jit(solution)/shard_map/transpose(jvp())/reduce_sum | solution.py:74
  66.2 2.3 multiply_reduce_fusion.16
  70.5 2.6 multiply_reduce_fusion.4
  73.1 2.8 pad_add_fusion
  76.7 2.1 convolution_convert_fusion
  84.2 2.5 convolution_convert_fusion.5
  87.0 1.3 convolution_convert_fusion.2
  88.7 1.7 convolution_convert_fusion.3
  90.6 2.3 convolution_convert_fusion.4
  92.8 1.1 copy.42
  93.9 1.8 scatter_custom_fusion
  95.8 1.0 all_to_all.25
  96.8 10.3 %all-to-all-start.1 = ((bf16[32,4,2304]{2,1,0:T(4,128)(2,1)}), bf16[32,4,2304]{2,1,0:T(4,128)(2,1)S(1)}, u32[]{:S(2)}, u32[]{:S(2)}) async-start(bf16[32,4,2304]{2,1,0:T(4,128)(2,1)} %all_to_all.25), calls=%async_computation.1 | async-start | bytes 1179648 | tf_op jit(solution)/shard_map/all_to_all | solution.py:119
  107.2 2.4 multiply_reduce_fusion.22
  110.1 1.0 pad_add_fusion.7
  111.2 26.3 %reduce-scatter.2.cloned.1.call-done = bf16[48,1536]{1,0:T(8,128)(2,1)} async-done(((bf16[768,1536]{1,0:T(8,128)(2,1)}), bf16[48,1536]{1,0:T(8,128)(2,1)}) %reduce-scatter.2.cloned.1.call-update) | async-done | bytes 147472 | tf_op jit(solution)/shard_map/reduce_scatter | solution.py:101
  138.4 112.9 %all-reduce.66.cloned.1.call-done = f32[31,1536]{1,0:T(8,128)} async-done(((f32[31,1536]{1,0:T(8,128)}), f32[31,1536]{1,0:T(8,128)}) %all-reduce.66.cloned.1.call-update) | async-done | bytes 190480 | tf_op jit(solution)/shard_map/psum | solution.py:123
  251.3 1.0 maximum_maximum_fusion
  252.3 1.5 all_to_all.30
  253.8 10.2 %all-to-all-start.2 = ((f32[32,1,4608]{2,1,0:T(1,128)}), f32[32,1,4608]{2,1,0:T(1,128)S(1)}, u32[]{:S(2)}, u32[]{:S(2)}) async-start(f32[32,1,4608]{2,1,0:T(1,128)} %all_to_all.30), calls=%async_computation.3 | async-start | bytes 1179648 | tf_op jit(solution)/shard_map/all_to_all | solution.py:146
  264.2 2.4 scatter_custom_fusion.1
  266.6 17.0 %all-to-all-done.2 = f32[32,1,4608]{2,1,0:T(1,128)S(1)} async-done(((f32[32,1,4608]{2,1,0:T(1,128)}), f32[32,1,4608]{2,1,0:T(1,128)S(1)}, u32[]{:S(2)}, u32[]{:S(2)}) %all-to-all-start.2) | async-done | bytes 589856 | tf_op jit(solution)/shard_map/all_to_all | solution.py:146
  283.9 48.8 %all-gather.1 = f32[32,1,4608]{2,1,0:T(1,128)S(1)} all-gather(f32[1,1,4608]{2,1,0:T(1,128)S(1)} %reshape.348), channel_id=2, replica_groups=mesh['dp'=32,'fsdp'=16] {'dp'}, dimensions={0}, use_global_device_ids=true | all-gather | bytes 608256 | tf_op jit(solution)/shard_map/all_gather | solution.py:148
  (176 shorter events, 16.5 us)
Async XLA Ops:
  7.2 49.2 %all-gather.4.cloned.1.call-start = ((), (), s32[]{:S(2)}) async-start(), calls=%async_computation.4 | async-start | bytes 2506752 | tf_op jit(solution)/shard_map/all_gather | solution.py:92
  10.1 14.4 %copy-start.6 = (f32[31,1536]{1,0:T(8,128)S(1)}, f32[31,1536]{1,0:T(8,128)}, u32[]{:S(2)}) copy-start(f32[31,1536]{1,0:T(8,128)} %param.11) | copy-start | bytes 571396
  10.1 14.6 %copy-start.48 = (s32[128]{0:T(128)S(1)}, s32[128]{0:T(128)}, u32[]{:S(2)}) copy-start(s32[128]{0:T(128)} %param.14) | copy-start | bytes 1540
  10.1 15.5 %copy-start.46 = (s32[128]{0:T(128)S(1)}, s32[128]{0:T(128)}, u32[]{:S(2)}) copy-start(s32[128]{0:T(128)} %param.15) | copy-start | bytes 1540
  11.3 32.2 %all-to-all-start = ((bf16[32,4,2304]{2,1,0:T(4,128)(2,1)}), bf16[32,4,2304]{2,1,0:T(4,128)(2,1)S(1)}, u32[]{:S(2)}, u32[]{:S(2)}) async-start(bf16[32,4,2304]{2,1,0:T(4,128)(2,1)} %all_to_all.22), calls=%async_computation | async-start | bytes 1179648 | tf_op jit(solution)/shard_map/all_to_all | solution.py:84
  24.4 113.0 %reduce-scatter.2.cloned.1.call-start = ((), (), s32[]{:S(2)}) async-start(), calls=%async_computation.5 | async-start | bytes 2506752 | tf_op jit(solution)/shard_map/reduce_scatter | solution.py:101
  25.8 43.2 %copy-start.43 = (f32[128]{0:T(128)}, f32[128]{0:T(128)S(1)}, u32[]{:S(2)}) copy-start(f32[128]{0:T(128)S(1)} %get-tuple-element.120) | copy-start | bytes 1540
  25.8 43.2 %copy-start.44 = (f32[128]{0:T(128)}, f32[128]{0:T(128)S(1)}, u32[]{:S(2)}) copy-start(f32[128]{0:T(128)S(1)} %get-tuple-element.121) | copy-start | bytes 1540
  25.8 43.2 %copy-start.45 = (f32[128]{0:T(128)}, f32[128]{0:T(128)S(1)}, u32[]{:S(2)}) copy-start(f32[128]{0:T(128)S(1)} %get-tuple-element.122) | copy-start | bytes 1540
  25.8 43.9 %copy-start.37 = (f32[128]{0:T(128)}, f32[128]{0:T(128)S(1)}, u32[]{:S(2)}) copy-start(f32[128]{0:T(128)S(1)} %get-tuple-element.114) | copy-start | bytes 1540
  25.8 43.9 %copy-start.38 = (f32[128]{0:T(128)}, f32[128]{0:T(128)S(1)}, u32[]{:S(2)}) copy-start(f32[128]{0:T(128)S(1)} %get-tuple-element.115) | copy-start | bytes 1540
  25.8 43.9 %copy-start.39 = (f32[128]{0:T(128)}, f32[128]{0:T(128)S(1)}, u32[]{:S(2)}) copy-start(f32[128]{0:T(128)S(1)} %get-tuple-element.116) | copy-start | bytes 1540
  25.9 43.9 %copy-start.40 = (f32[128]{0:T(128)}, f32[128]{0:T(128)S(1)}, u32[]{:S(2)}) copy-start(f32[128]{0:T(128)S(1)} %get-tuple-element.117) | copy-start | bytes 1540
  25.9 43.9 %copy-start.41 = (f32[128]{0:T(128)}, f32[128]{0:T(128)S(1)}, u32[]{:S(2)}) copy-start(f32[128]{0:T(128)S(1)} %get-tuple-element.118) | copy-start | bytes 1540
  25.9 43.9 %copy-start.42 = (f32[128]{0:T(128)}, f32[128]{0:T(128)S(1)}, u32[]{:S(2)}) copy-start(f32[128]{0:T(128)S(1)} %get-tuple-element.119) | copy-start | bytes 1540
  26.0 20.5 %copy-start.36 = (pred[128,128]{0,1:T(8,128)(4,1)}, pred[128,128]{0,1:T(8,128)(4,1)S(1)}, u32[]{:S(2)}) copy-start(pred[128,128]{0,1:T(8,128)(4,1)S(1)} %broadcast_compare_fusion) | copy-start | bytes 49156
  44.9 42.0 %copy-start.2 = (bf16[128,768]{0,1:T(8,128)(2,1)}, bf16[128,768]{0,1:T(8,128)(2,1)S(1)}, u32[]{:S(2)}) copy-start(bf16[128,768]{0,1:T(8,128)(2,1)S(1)} %copy.36) | copy-start | bytes 589828
  95.7 14.1 %copy-start.10 = (f32[1536]{0:T(1024)S(1)}, f32[1536]{0:T(1024)}, u32[]{:S(2)}) copy-start(f32[1536]{0:T(1024)} %get-tuple-element.26) | copy-start | bytes 18436
  95.7 14.1 %copy-start.9 = (f32[1536]{0:T(1024)S(1)}, f32[1536]{0:T(1024)}, u32[]{:S(2)}) copy-start(f32[1536]{0:T(1024)} %get-tuple-element.27) | copy-start | bytes 18436
  95.7 14.1 %copy-start.8 = (f32[1536]{0:T(1024)S(1)}, f32[1536]{0:T(1024)}, u32[]{:S(2)}) copy-start(f32[1536]{0:T(1024)} %get-tuple-element.28) | copy-start | bytes 18436
  95.7 14.1 %copy-start.7 = (f32[1536]{0:T(1024)S(1)}, f32[1536]{0:T(1024)}, u32[]{:S(2)}) copy-start(f32[1536]{0:T(1024)} %get-tuple-element.29) | copy-start | bytes 18436
  95.7 14.1 %copy-start.17 = (f32[1536]{0:T(1024)S(1)}, f32[1536]{0:T(1024)}, u32[]{:S(2)}) copy-start(f32[1536]{0:T(1024)} %get-tuple-element.32) | copy-start | bytes 18436
  95.7 14.2 %copy-start.16 = (f32[1536]{0:T(1024)S(1)}, f32[1536]{0:T(1024)}, u32[]{:S(2)}) copy-start(f32[1536]{0:T(1024)} %get-tuple-element.33) | copy-start | bytes 18436
  95.8 14.2 %copy-start.15 = (f32[1536]{0:T(1024)S(1)}, f32[1536]{0:T(1024)}, u32[]{:S(2)}) copy-start(f32[1536]{0:T(1024)} %get-tuple-element.34) | copy-start | bytes 18436
  95.8 14.2 %copy-start.14 = (f32[1536]{0:T(1024)S(1)}, f32[1536]{0:T(1024)}, u32[]{:S(2)}) copy-start(f32[1536]{0:T(1024)} %get-tuple-element.35) | copy-start | bytes 18436
  95.8 14.2 %copy-start.27 = (f32[1,1536]{1,0:T(1,128)S(1)}, f32[1,1536]{1,0:T(1,128)}, u32[]{:S(2)}) copy-start(f32[1,1536]{1,0:T(1,128)} %reshape.271) | copy-start | bytes 18436
  95.8 14.2 %copy-start.28 = (f32[1,1536]{1,0:T(1,128)S(1)}, f32[1,1536]{1,0:T(1,128)}, u32[]{:S(2)}) copy-start(f32[1,1536]{1,0:T(1,128)} %reshape.272) | copy-start | bytes 18436
  95.8 14.2 %copy-start.29 = (f32[1,1536]{1,0:T(1,128)S(1)}, f32[1,1536]{1,0:T(1,128)}, u32[]{:S(2)}) copy-start(f32[1,1536]{1,0:T(1,128)} %reshape.273) | copy-start | bytes 18436
  95.8 14.2 %copy-start.30 = (f32[1,1536]{1,0:T(1,128)S(1)}, f32[1,1536]{1,0:T(1,128)}, u32[]{:S(2)}) copy-start(f32[1,1536]{1,0:T(1,128)} %reshape.274) | copy-start | bytes 18436
  96.8 157.1 %all-to-all-start.1 = ((bf16[32,4,2304]{2,1,0:T(4,128)(2,1)}), bf16[32,4,2304]{2,1,0:T(4,128)(2,1)S(1)}, u32[]{:S(2)}, u32[]{:S(2)}) async-start(bf16[32,4,2304]{2,1,0:T(4,128)(2,1)} %all_to_all.25), calls=%async_computation.1 | async-start | bytes 1179648 | tf_op jit(solution)/shard_map/all_to_all | solution.py:119
  107.1 144.2 %all-reduce.66.cloned.1.call-start = ((), (), s32[]{:S(2)}) async-start(), calls=%async_computation.6 | async-start | bytes 393216 | tf_op jit(solution)/shard_map/psum | solution.py:123
  253.8 29.7 %all-to-all-start.2 = ((f32[32,1,4608]{2,1,0:T(1,128)}), f32[32,1,4608]{2,1,0:T(1,128)S(1)}, u32[]{:S(2)}, u32[]{:S(2)}) async-start(f32[32,1,4608]{2,1,0:T(1,128)} %all_to_all.30), calls=%async_computation.3 | async-start | bytes 1179648 | tf_op jit(solution)/shard_map/all_to_all | solution.py:146
  (25 other events, 198.5 us)
Sparse Core Ops, SparseCore 0:
  10.1 46.2 all-gather.3
  78.9 58.4 reduce-scatter.1
  140.4 110.8 all-reduce.65
where the time goes:
time: 342 us
  waiting for transfers between devices  184 us (54%)
  blocking collectives  48.8 us (14%)
  starting transfers between devices  33.8 us (10%)
  other arithmetic  28.4 us (8%)
  local copies, waits for them, and re-layouts  17.9 us (5%)
  between operations  14.9 us (4%)
  matrix products  14 us (4%)
    psum x1, waiting for transfers between devices, body(): kernel_f = lax.psum(kernel_part, 'fsdp')  113 us
    all_gather x1, blocking collectives, dp_allreduce_a2a(): return lax.all_gather(part, 'dp', axis=0, tiled=True).reshape(x.shape)  48.8 us
    reduce_scatter x1, waiting for transfers between devices, body(): lax.psum_scatter(jnp.einsum('rc,rd->cd', columns, mixed_grad, preferred_e...  26.3 us
    all_to_all x1, waiting for transfers between devices, body(): lax.all_to_all(outgoing, 'dp', split_axis=0, concat_axis=0, tiled=True)  17.5 us
    all_to_all x1, waiting for transfers between devices, dp_allreduce_a2a(): got = lax.all_to_all(flat, 'dp', split_axis=0, concat_axis=0, tiled=True)  17 us
    reduce_sum x4, other arithmetic, finish(): kernel[offset] * padded[offset:offset + length] * matching[:, None]  14.9 us
    all_to_all x1, starting transfers between devices, body(): lax.all_to_all(outgoing, 'dp', split_axis=0, concat_axis=0, tiled=True)  13.2 us
    all_to_all x1, starting transfers between devices, body(): lax.all_to_all(returning, 'dp', split_axis=0, concat_axis=0, tiled=True)  10.3 us
  transfers between devices with their start and end apart: 6, of which 5 were waited for; matrix products, arithmetic and copies ran while one was open for 9% of the time, Pallas kernels for 0%

commit v1 on v0

--- a/solution.py
+++ b/solution.py
@@ -89,7 +89,9 @@
     columns = context
     mixed_sums = jnp.dot(
         columns,
-        lax.all_gather(out_weight, "fsdp", axis=0, tiled=True),
+        jnp.concatenate(
+            lax.all_to_all(jnp.stack([out_weight] * lax.axis_size("fsdp")), "fsdp", 0, 0), axis=0
+        ),
         preferred_element_type=jnp.float32,
     )
     mixed = mixed_sums.astype(jnp.bfloat16)

time: 342 us -> 396 us (1.16)
  waiting for transfers between devices: 184 us -> 221 us
  blocking collectives: 48.8 us -> 80.8 us
  starting transfers between devices: 33.8 us -> 21.9 us
  local copies, waits for them, and re-layouts: 17.9 us -> 13.3 us
    all_to_all x1, waiting for transfers between devices: 17.5 us -> 58.3 us  [body(): lax.all_to_all(jnp.stack([out_weight] * lax.axis_size('fsdp')), 'fsdp', 0...]
    all_to_all x0 -> x1, blocking collectives: none -> 32 us  [body(): lax.all_to_all(outgoing, 'dp', split_axis=0, concat_axis=0, tiled=True)]
    all_gather x1, waiting for transfers between devices: 9.41 us -> 0.02 us  [body(): lax.all_gather(out_weight, 'fsdp', axis=0, tiled=True)]
    reduce_scatter x1, waiting for transfers between devices: 26.3 us -> 32.8 us  [body(): lax.psum_scatter(jnp.einsum('rc,rd->cd', columns, mixed_grad, preferred_e...]
    all_to_all x1, starting transfers between devices: 10.3 us -> 4.18 us  [body(): lax.all_to_all(returning, 'dp', split_axis=0, concat_axis=0, tiled=True)]
    all_to_all x1, starting transfers between devices: 13.2 us -> 7.47 us  [body(): lax.all_to_all(jnp.stack([out_weight] * lax.axis_size('fsdp')), 'fsdp', 0...]
    reshape x31, local copies, waits for them, and re-layouts: 5.52 us -> 0.2 us  [finish(): kernel[offset] * padded[offset:offset + length] * matching[:, None]]
  transfers between devices with their start and end apart: 6 -> 6, of which waited for: 5 -> 4; matrix products, arithmetic and copies ran while one was open for 9% -> 12% of each run, Pallas kernels for 0% -> 0%
where the time goes in v1:
time: 396 us; the launch traced here: 395 us
  waiting for transfers between devices  221 us (56%)
  blocking collectives  80.8 us (20%)
  other arithmetic  29.1 us (7%)
  starting transfers between devices  21.9 us (6%)
  between operations  14.9 us (4%)
  matrix products  14.1 us (4%)
  local copies, waits for them, and re-layouts  13.3 us (3%)
    psum x1, waiting for transfers between devices, body(): kernel_f = lax.psum(kernel_part, 'fsdp')  113 us
    all_to_all x1, waiting for transfers between devices, body(): lax.all_to_all(jnp.stack([out_weight] * lax.axis_size('fsdp')), 'fsdp', 0...  58.3 us
    all_gather x1, blocking collectives, dp_allreduce_a2a(): return lax.all_gather(part, 'dp', axis=0, tiled=True).reshape(x.shape)  48.8 us
    reduce_scatter x1, waiting for transfers between devices, body(): lax.psum_scatter(jnp.einsum('rc,rd->cd', columns, mixed_grad, preferred_e...  32.8 us
    all_to_all x1, blocking collectives, body(): lax.all_to_all(outgoing, 'dp', split_axis=0, concat_axis=0, tiled=True)  32 us
    all_to_all x1, waiting for transfers between devices, dp_allreduce_a2a(): got = lax.all_to_all(flat, 'dp', split_axis=0, concat_axis=0, tiled=True)  17 us
    reduce_sum x4, other arithmetic, finish(): kernel[offset] * padded[offset:offset + length] * matching[:, None]  14.8 us
    all_to_all x1, starting transfers between devices, dp_allreduce_a2a(): got = lax.all_to_all(flat, 'dp', split_axis=0, concat_axis=0, tiled=True)  10.2 us
  transfers between devices with their start and end apart: 6, of which 4 were waited for; matrix products, arithmetic and copies ran while one was open for 12% of the time, Pallas kernels for 0%

profile of v1, /device:TPU:24, one launch (start us, length us, event | category | flops | bytes accessed | tf_op | source)
XLA Modules:
  0.0 395.5 jit_solution(7598536106117692705)
XLA Ops:
  7.2 1.3 compare_select_fusion.1
  9.1 1.0 gather_fusion
  10.4 32.0 %all_to_all.39 = bf16[32,4,2304]{2,1,0:T(4,128)(2,1)S(1)} all-to-all(bf16[32,4,2304]{2,1,0:T(4,128)(2,1)S(1)} %all_to_all.25), channel_id=1, replica_groups=mesh['dp'=32,'fsdp'=16] {'dp'}, dimensions={0} | all-to-all | bytes 1179648 | tf_op jit(solution)/shard_map/all_to_all | solution.py:84
  42.4 1.7 stack.2
  44.1 7.5 %all-to-all-start.1 = ((bf16[16,48,1536]{2,1,0:T(8,128)(2,1)}), bf16[16,48,1536]{2,1,0:T(8,128)(2,1)}, u32[]{:S(2)}, u32[]{:S(2)}) async-start(bf16[16,48,1536]{2,1,0:T(8,128)(2,1)} %stack.2), calls=%async_computation.1 | async-start | bytes 4718592 | tf_op jit(solution)/shard_map/all_to_all | solution.py:93
  53.9 1.0 gather_fusion.1
  55.6 1.2 fusion.40
  57.3 58.3 %all-to-all-done.1 = bf16[16,48,1536]{2,1,0:T(8,128)(2,1)} async-done(((bf16[16,48,1536]{2,1,0:T(8,128)(2,1)}), bf16[16,48,1536]{2,1,0:T(8,128)(2,1)}, u32[]{:S(2)}, u32[]{:S(2)}) %all-to-all-start.1) | async-done | bytes 2359328 | tf_op jit(solution)/shard_map/all_to_all | solution.py:93
  115.6 2.2 fusion.2
  117.8 7.6 %multiply_reduce_fusion.31 = (f32[1536]{0:T(1024)}, f32[1536]{0:T(1024)}, f32[1536]{0:T(1024)}, f32[1536]{0:T(1024)}, f32[1536]{0:T(1024)}, /*index=5*/f32[1536]...) fusion(f32[128,1536]{1,0:T(8,128)S(1)} %fusion.2, ...), kind=kLoop, calls=%fused_computation.99 | loop fusion | flops 25152000 | bytes 3013632 | tf_op jit(solution)/shard_map/transpose(jvp())/reduce_sum | solution.py:74
  125.4 2.3 multiply_reduce_fusion.16
  127.7 2.6 multiply_reduce_fusion.4
  132.4 2.8 pad_add_fusion
  135.8 2.2 convolution_convert_fusion
  138.1 2.5 convolution_convert_fusion.5
  141.1 1.6 convolution_convert_fusion.4
  142.8 2.2 convolution_convert_fusion.3
  145.0 1.1 copy.43
  146.1 1.5 convolution_convert_fusion.2
  147.7 1.8 scatter_custom_fusion
  149.7 1.0 all_to_all.29
  150.6 4.2 %all-to-all-start.2 = ((bf16[32,4,2304]{2,1,0:T(4,128)(2,1)}), bf16[32,4,2304]{2,1,0:T(4,128)(2,1)S(1)}, u32[]{:S(2)}, u32[]{:S(2)}) async-start(bf16[32,4,2304]{2,1,0:T(4,128)(2,1)} %all_to_all.29), calls=%async_computation.2 | async-start | bytes 1179648 | tf_op jit(solution)/shard_map/all_to_all | solution.py:121
  154.9 2.3 multiply_reduce_fusion.22
  157.9 1.0 pad_add_fusion.7
  159.0 32.8 %reduce-scatter.2.cloned.1.call-done = bf16[48,1536]{1,0:T(8,128)(2,1)} async-done(((bf16[768,1536]{1,0:T(8,128)(2,1)}), bf16[48,1536]{1,0:T(8,128)(2,1)}) %reduce-scatter.2.cloned.1.call-update) | async-done | bytes 147472 | tf_op jit(solution)/shard_map/reduce_scatter | solution.py:103
  192.7 112.5 %all-reduce.66.cloned.1.call-done = f32[31,1536]{1,0:T(8,128)} async-done(((f32[31,1536]{1,0:T(8,128)}), f32[31,1536]{1,0:T(8,128)}) %all-reduce.66.cloned.1.call-update) | async-done | bytes 190480 | tf_op jit(solution)/shard_map/psum | solution.py:125
  305.2 1.0 maximum_maximum_fusion
  306.3 1.5 all_to_all.34
  307.8 10.2 %all-to-all-start.3 = ((f32[32,1,4608]{2,1,0:T(1,128)}), f32[32,1,4608]{2,1,0:T(1,128)S(1)}, u32[]{:S(2)}, u32[]{:S(2)}) async-start(f32[32,1,4608]{2,1,0:T(1,128)} %all_to_all.34), calls=%async_computation.4 | async-start | bytes 1179648 | tf_op jit(solution)/shard_map/all_to_all | solution.py:148
  318.1 2.4 scatter_custom_fusion.1
  320.5 17.0 %all-to-all-done.3 = f32[32,1,4608]{2,1,0:T(1,128)S(1)} async-done(((f32[32,1,4608]{2,1,0:T(1,128)}), f32[32,1,4608]{2,1,0:T(1,128)S(1)}, u32[]{:S(2)}, u32[]{:S(2)}) %all-to-all-start.3) | async-done | bytes 589856 | tf_op jit(solution)/shard_map/all_to_all | solution.py:148
  337.8 48.8 %all-gather.1 = f32[32,1,4608]{2,1,0:T(1,128)S(1)} all-gather(f32[1,1,4608]{2,1,0:T(1,128)S(1)} %reshape.355), channel_id=2, replica_groups=mesh['dp'=32,'fsdp'=16] {'dp'}, dimensions={0}, use_global_device_ids=true | all-gather | bytes 608256 | tf_op jit(solution)/shard_map/all_gather | solution.py:150
  (156 shorter events, 11.9 us)
Async XLA Ops:
  10.1 32.3 %copy-start.2 = (bf16[48,1536]{1,0:T(8,128)(2,1)S(1)}, bf16[48,1536]{1,0:T(8,128)(2,1)}, u32[]{:S(2)}) copy-start(bf16[48,1536]{1,0:T(8,128)(2,1)} %param.10) | copy-start | bytes 442372
  44.1 8.3 %copy-start.37 = (s32[128]{0:T(128)S(1)}, s32[128]{0:T(128)}, u32[]{:S(2)}) copy-start(s32[128]{0:T(128)} %param.14) | copy-start | bytes 1540
  44.1 8.8 %copy-start.6 = (f32[31,1536]{1,0:T(8,128)S(1)}, f32[31,1536]{1,0:T(8,128)}, u32[]{:S(2)}) copy-start(f32[31,1536]{1,0:T(8,128)} %param.11) | copy-start | bytes 571396
  44.1 9.3 %copy-start.36 = (s32[128]{0:T(128)S(1)}, s32[128]{0:T(128)}, u32[]{:S(2)}) copy-start(s32[128]{0:T(128)} %param.15) | copy-start | bytes 1540
  44.1 71.6 %all-to-all-start.1 = ((bf16[16,48,1536]{2,1,0:T(8,128)(2,1)}), bf16[16,48,1536]{2,1,0:T(8,128)(2,1)}, u32[]{:S(2)}, u32[]{:S(2)}) async-start(bf16[16,48,1536]{2,1,0:T(8,128)(2,1)} %stack.2), calls=%async_computation.1 | async-start | bytes 4718592 | tf_op jit(solution)/shard_map/all_to_all | solution.py:93
  51.5 86.5 %all-gather.4.cloned.1.call-start = ((), (), s32[]{:S(2)}) async-start(), calls=%async_computation.5 | async-start | bytes 2506752 | tf_op jit(solution)/shard_map/all_gather | solution.py:114
  52.3 139.5 %reduce-scatter.2.cloned.1.call-start = ((), (), s32[]{:S(2)}) async-start(), calls=%async_computation.6 | async-start | bytes 2506752 | tf_op jit(solution)/shard_map/reduce_scatter | solution.py:103
  53.6 77.2 %copy-start.27 = (f32[128]{0:T(128)}, f32[128]{0:T(128)S(1)}, u32[]{:S(2)}) copy-start(f32[128]{0:T(128)S(1)} %get-tuple-element.114) | copy-start | bytes 1540
  53.6 77.2 %copy-start.28 = (f32[128]{0:T(128)}, f32[128]{0:T(128)S(1)}, u32[]{:S(2)}) copy-start(f32[128]{0:T(128)S(1)} %get-tuple-element.115) | copy-start | bytes 1540
  53.6 77.2 %copy-start.29 = (f32[128]{0:T(128)}, f32[128]{0:T(128)S(1)}, u32[]{:S(2)}) copy-start(f32[128]{0:T(128)S(1)} %get-tuple-element.116) | copy-start | bytes 1540
  53.6 77.2 %copy-start.30 = (f32[128]{0:T(128)}, f32[128]{0:T(128)S(1)}, u32[]{:S(2)}) copy-start(f32[128]{0:T(128)S(1)} %get-tuple-element.117) | copy-start | bytes 1540
  53.6 77.2 %copy-start.31 = (f32[128]{0:T(128)}, f32[128]{0:T(128)S(1)}, u32[]{:S(2)}) copy-start(f32[128]{0:T(128)S(1)} %get-tuple-element.118) | copy-start | bytes 1540
  53.6 77.2 %copy-start.32 = (f32[128]{0:T(128)}, f32[128]{0:T(128)S(1)}, u32[]{:S(2)}) copy-start(f32[128]{0:T(128)S(1)} %get-tuple-element.119) | copy-start | bytes 1540
  53.6 77.9 %copy-start.33 = (f32[128]{0:T(128)}, f32[128]{0:T(128)S(1)}, u32[]{:S(2)}) copy-start(f32[128]{0:T(128)S(1)} %get-tuple-element.120) | copy-start | bytes 1540
  53.7 77.9 %copy-start.34 = (f32[128]{0:T(128)}, f32[128]{0:T(128)S(1)}, u32[]{:S(2)}) copy-start(f32[128]{0:T(128)S(1)} %get-tuple-element.121) | copy-start | bytes 1540
  53.7 77.9 %copy-start.35 = (f32[128]{0:T(128)}, f32[128]{0:T(128)S(1)}, u32[]{:S(2)}) copy-start(f32[128]{0:T(128)S(1)} %get-tuple-element.122) | copy-start | bytes 1540
  55.4 60.2 %copy-start.5 = (bf16[128,768]{0,1:T(8,128)(2,1)}, bf16[128,768]{0,1:T(8,128)(2,1)S(1)}, u32[]{:S(2)}) copy-start(bf16[128,768]{0,1:T(8,128)(2,1)S(1)} %copy.36) | copy-start | bytes 589828
  56.8 61.1 %copy-start.38 = (f32[8,128]{1,0:T(8,128)}, f32[8,128]{1,0:T(8,128)S(1)}, u32[]{:S(2)}) copy-start(f32[8,128]{1,0:T(8,128)S(1)} %get-tuple-element.142) | copy-start | bytes 12292
  57.3 60.5 %copy-start.1 = (bf16[128,1536]{1,0:T(8,128)(2,1)S(1)}, bf16[128,1536]{1,0:T(8,128)(2,1)}, u32[]{:S(2)}) copy-start(bf16[128,1536]{1,0:T(8,128)(2,1)} %param.12) | copy-start | bytes 1179652
  149.6 8.0 %copy-start.23 = (f32[1536]{0:T(1024)S(1)}, f32[1536]{0:T(1024)}, u32[]{:S(2)}) copy-start(f32[1536]{0:T(1024)} %get-tuple-element.33) | copy-start | bytes 18436
  149.6 8.0 %copy-start.21 = (f32[1536]{0:T(1024)S(1)}, f32[1536]{0:T(1024)}, u32[]{:S(2)}) copy-start(f32[1536]{0:T(1024)} %get-tuple-element.34) | copy-start | bytes 18436
  149.6 8.0 %copy-start.19 = (f32[1536]{0:T(1024)S(1)}, f32[1536]{0:T(1024)}, u32[]{:S(2)}) copy-start(f32[1536]{0:T(1024)} %get-tuple-element.35) | copy-start | bytes 18436
  149.6 8.0 %copy-start.13 = (f32[1536]{0:T(1024)S(1)}, f32[1536]{0:T(1024)}, u32[]{:S(2)}) copy-start(f32[1536]{0:T(1024)} %get-tuple-element.5) | copy-start | bytes 18436
  149.6 8.1 %copy-start.12 = (f32[1536]{0:T(1024)S(1)}, f32[1536]{0:T(1024)}, u32[]{:S(2)}) copy-start(f32[1536]{0:T(1024)} %get-tuple-element.6) | copy-start | bytes 18436
  149.6 8.1 %copy-start.11 = (f32[1536]{0:T(1024)S(1)}, f32[1536]{0:T(1024)}, u32[]{:S(2)}) copy-start(f32[1536]{0:T(1024)} %get-tuple-element.7) | copy-start | bytes 18436
  149.7 8.1 %copy-start.10 = (f32[1536]{0:T(1024)S(1)}, f32[1536]{0:T(1024)}, u32[]{:S(2)}) copy-start(f32[1536]{0:T(1024)} %get-tuple-element.8) | copy-start | bytes 18436
  149.7 8.1 %copy-start.9 = (f32[1536]{0:T(1024)S(1)}, f32[1536]{0:T(1024)}, u32[]{:S(2)}) copy-start(f32[1536]{0:T(1024)} %get-tuple-element.9) | copy-start | bytes 18436
  149.7 8.1 %copy-start.8 = (f32[1536]{0:T(1024)S(1)}, f32[1536]{0:T(1024)}, u32[]{:S(2)}) copy-start(f32[1536]{0:T(1024)} %get-tuple-element.10) | copy-start | bytes 18436
  149.7 8.1 %copy-start.7 = (f32[1536]{0:T(1024)S(1)}, f32[1536]{0:T(1024)}, u32[]{:S(2)}) copy-start(f32[1536]{0:T(1024)} %get-tuple-element.11) | copy-start | bytes 18436
  150.6 157.1 %all-to-all-start.2 = ((bf16[32,4,2304]{2,1,0:T(4,128)(2,1)}), bf16[32,4,2304]{2,1,0:T(4,128)(2,1)S(1)}, u32[]{:S(2)}, u32[]{:S(2)}) async-start(bf16[32,4,2304]{2,1,0:T(4,128)(2,1)} %all_to_all.29), calls=%async_computation.2 | async-start | bytes 1179648 | tf_op jit(solution)/shard_map/all_to_all | solution.py:121
  154.8 150.4 %all-reduce.66.cloned.1.call-start = ((), (), s32[]{:S(2)}) async-start(), calls=%async_computation.7 | async-start | bytes 393216 | tf_op jit(solution)/shard_map/psum | solution.py:125
  307.8 29.7 %all-to-all-start.3 = ((f32[32,1,4608]{2,1,0:T(1,128)}), f32[32,1,4608]{2,1,0:T(1,128)S(1)}, u32[]{:S(2)}, u32[]{:S(2)}) async-start(f32[32,1,4608]{2,1,0:T(1,128)} %all_to_all.34), calls=%async_computation.4 | async-start | bytes 1179648 | tf_op jit(solution)/shard_map/all_to_all | solution.py:148
  (14 other events, 88.4 us)
Sparse Core Ops, SparseCore 0:
  54.5 65.3 all-gather.3
  138.1 53.5 reduce-scatter.1
  194.7 110.4 all-reduce.65
